TPU v7x, 32 devices: a whole 2x2x4 slice. The times are simulated.
32 devices in a mesh: groups: 2 (over y), picks: 4 (over z), heads: 4 (over x, core).
Axes of the slice: x: 2, y: 2, z: 4, core: 2. Of those that a mesh axis runs over, the one named last changes fastest.
Arguments:
- coords: float32 [3, 8192], P(None, ('groups', 'picks')), parts along dimension 1, may hold values from -1 to 1
- horizon_ids: int32 [8192], P(('groups', 'picks')), parts along dimension 0, may hold values from 0 to 63
- horizon_levels: float32 [128], P('groups'), parts along dimension 0, may hold values from -2 to 2
- latents: bfloat16 [512, 1024], replicated, may hold values from -960 to 960
- kv_weight: bfloat16 [3072, 2, 1024], P('picks', None, 'heads'), may hold values from -0.109375 to 0.109375
- cross_out: bfloat16 [1024, 1024], P('heads'), may hold values from -0.75 to 0.75
- norm_gains: float32 [2, 1024], replicated, may hold values from 0.1 to 1.9
- self_qkv: bfloat16 [3, 1024, 1024], P(None, None, 'heads'), may hold values from -0.1875 to 0.1875
- self_out: bfloat16 [1024, 1024], P(None, 'heads'), may hold values from -0.1875 to 0.1875
- dec_kv: bfloat16 [2, 1024, 1024], P(None, None, 'heads'), may hold values from -0.1875 to 0.1875
- dec_query: bfloat16 [3072, 1024], P('picks', 'heads'), may hold values from -0.109375 to 0.109375
- readout: float32 [1024], P('heads'), may hold values from -0.1875 to 0.1875
Outputs:
- field: float32 [8192], P(('groups', 'picks')), parts along dimension 0
- latents_out: float32 [1024, 1024], P('groups', 'heads'), parts along dimension 0
- grad_query: float32 [6144, 1024], P(('groups', 'picks'), 'heads'), parts along dimension 0
There are 2 independent parts, one for each index of `groups`. A program takes and returns all parts, laid end to end along the dimension named above; an argument that names none is the same for every part. Nothing has to cross between parts.
All inputs are finite; a program needn't handle non-finite values.
Results may differ from a plain program's by a relative error of at most 0.028.
Values may be sent and summed in bfloat16 or wider, within the bound.
No kernel may reach another device: no remote copies, remote signals or barrier semaphores. Data moves between devices by JAX's collectives and lax.ppermute only.
A program may use at most 64 MiB of HBM per device.

v0:
```python
import functools
import jax
import jax.numpy as jnp
from jax import lax
from jax.sharding import PartitionSpec as P

HEAD = 128
BANDS = 512
HORIZONS = 64
PI = 3.141592653589793
EPS = 1e-06
RING_MAX = 4


def encode(coords):
    freq = jnp.linspace(1.0, BANDS / 2.0, BANDS).astype(jnp.float32)
    angle = PI * freq[None, :, None] * coords[:, None, :]
    table = jnp.concatenate([jnp.sin(angle), jnp.cos(angle)], axis=0)
    return table.reshape(6 * BANDS, coords.shape[1]).T.astype(jnp.bfloat16)


def ring_gather(x, axis, n):
    if n == 1:
        return x
    if n > RING_MAX:
        return lax.all_gather(x, axis, axis=0, tiled=True)
    idx = lax.axis_index(axis)
    blocks = [x]
    for s in range(1, n):
        blocks.append(lax.ppermute(x, axis, [(i, (i - s) % n) for i in range(n)]))
    flipped = jnp.stack(blocks)
    ordered = jnp.roll(flipped, idx, axis=0)
    return ordered.reshape((n * x.shape[0],) + x.shape[1:])


def fetch_rows(kv_weight, n_picks, n_groups):
    if n_groups != 2:
        return lax.all_gather(kv_weight, "picks", axis=0, tiled=True)
    g = lax.axis_index("groups")
    rows = kv_weight.shape[0] // 2
    mine = lax.dynamic_slice_in_dim(kv_weight, g * rows, rows, 0)
    first = max(8, 2 * rows // 3 // 8 * 8)
    bounds = [(0, first), (first, rows)] if first < rows else [(0, rows)]
    own, other = ([], [])
    for lo, hi in bounds:
        gathered = lax.all_gather(mine[lo:hi], "picks", axis=0, tiled=False)
        own.append(gathered)
        other.append(lax.ppermute(gathered, "groups", [(0, 1), (1, 0)]))
    halves = jnp.stack([jnp.concatenate(own, axis=1), jnp.concatenate(other, axis=1)], axis=1)
    halves = jnp.roll(halves, g, axis=1)
    return halves.reshape((n_picks * kv_weight.shape[0],) + kv_weight.shape[1:])


def pair_sum(x, axis, n):
    if n != 4:
        return lax.psum(x, axis)
    x = x + lax.ppermute(x, axis, [(k, k ^ 1) for k in range(n)])
    return x + lax.ppermute(x, axis, [(k, k ^ 2) for k in range(n)])


def on_device(
    coords,
    horizon_ids,
    horizon_levels,
    latents,
    kv_weight,
    cross_out,
    norm_gains,
    self_qkv,
    self_out,
    dec_kv,
    dec_query,
    readout,
    *,
    n_picks,
    n_heads,
    n_groups
):
    high = lax.Precision.HIGHEST
    scale = HEAD ** (-0.5)
    count = coords.shape[1]
    width = latents.shape[1]
    lat_rows = latents.shape[0]
    local = kv_weight.shape[2]
    nheads = local // HEAD
    column = lax.axis_index("heads") * local
    enc = encode(coords)
    cross_full = ring_gather(cross_out, "heads", n_heads)
    piece = lax.all_gather(kv_weight, "picks", axis=0, tiled=True)
    cross_full, piece = lax.optimization_barrier((cross_full, piece))
    keys_vals = jnp.einsum("tf,fjc->tjc", enc, piece, preferred_element_type=jnp.float32).astype(
        jnp.bfloat16
    )
    keys = keys_vals[:, 0].reshape(count, nheads, HEAD)
    values = keys_vals[:, 1].reshape(count, nheads, HEAD)
    queries = lax.dynamic_slice_in_dim(latents, column, local, 1).reshape(lat_rows, nheads, HEAD)
    scores = jnp.einsum("lhc,thc->hlt", queries, keys, preferred_element_type=jnp.float32) * scale
    top = jnp.max(scores, axis=2)
    expo = jnp.exp(scores - top[:, :, None])
    total = jnp.sum(expo, axis=2)
    numer = jnp.einsum(
        "hlt,thc->hlc", expo.astype(jnp.bfloat16), values, preferred_element_type=jnp.float32
    )
    all_numer = lax.all_gather(numer.astype(jnp.bfloat16), "picks", axis=0, tiled=False)
    all_stats = lax.all_gather(jnp.stack([top, total]), "picks", axis=0, tiled=False)
    best = jnp.max(all_stats[:, 0], axis=0)
    factor = jnp.exp(all_stats[:, 0] - best[None])
    merged_total = jnp.sum(factor * all_stats[:, 1], axis=0)
    merged_numer = jnp.einsum(
        "phl,phlc->hlc", factor, all_numer.astype(jnp.float32), precision=high
    )
    attended = (
        (merged_numer / merged_total[:, :, None])
        .transpose(1, 0, 2)
        .reshape(lat_rows, local)
        .astype(jnp.bfloat16)
    )
    out_full = ring_gather(self_out.T, "heads", n_heads).T
    out_full, attended = lax.optimization_barrier((out_full, attended))
    dq_local, attended = lax.optimization_barrier((dec_query, attended))
    dq_full = lax.all_gather(dq_local, "picks", axis=0, tiled=True)
    attended_full = ring_gather(attended.T, "heads", n_heads).T
    whole = latents.astype(jnp.float32) + jnp.dot(
        attended_full, cross_full, preferred_element_type=jnp.float32
    )
    power = jnp.mean(whole * whole, axis=1, keepdims=True)
    normed = (whole * lax.rsqrt(power + EPS) * norm_gains[0][None, :]).astype(jnp.bfloat16)
    state = lax.dynamic_slice_in_dim(whole, column, local, 1)
    qkv = jnp.einsum("ld,kde->kle", normed, self_qkv, preferred_element_type=jnp.float32).astype(
        jnp.bfloat16
    )
    self_q = qkv[0].reshape(lat_rows, nheads, HEAD)
    self_k = qkv[1].reshape(lat_rows, nheads, HEAD)
    self_v = qkv[2].reshape(lat_rows, nheads, HEAD)
    inner = jnp.einsum("lhc,mhc->hlm", self_q, self_k, preferred_element_type=jnp.float32) * scale
    raised = jnp.exp(inner)
    probs = (raised / jnp.sum(raised, axis=2, keepdims=True)).astype(jnp.bfloat16)
    head_out = (
        jnp.einsum("hlm,mhc->lhc", probs, self_v, preferred_element_type=jnp.float32)
        .astype(jnp.bfloat16)
        .reshape(lat_rows, local)
    )
    every_head = ring_gather(head_out.T, "heads", n_heads).T
    out_whole = whole + jnp.dot(every_head, out_full, preferred_element_type=jnp.float32)
    latents_out = lax.dynamic_slice_in_dim(out_whole, column, local, 1)
    power_two = jnp.mean(out_whole * out_whole, axis=1, keepdims=True)
    normed2 = (out_whole * lax.rsqrt(power_two + EPS) * norm_gains[1][None, :]).astype(jnp.bfloat16)
    dec = jnp.einsum("ld,kde->kle", normed2, dec_kv, preferred_element_type=jnp.float32).astype(
        jnp.bfloat16
    )
    dec_keys = dec[0].reshape(lat_rows, nheads, HEAD)
    dec_vals = dec[1].reshape(lat_rows, nheads, HEAD)
    query = jnp.dot(enc, dq_full, preferred_element_type=jnp.float32).astype(jnp.bfloat16)
    dec_q = query.reshape(count, nheads, HEAD)
    logits = jnp.einsum("thc,lhc->htl", dec_q, dec_keys, preferred_element_type=jnp.float32) * scale
    lifted = jnp.exp(logits)
    weights = lifted / jnp.sum(lifted, axis=2, keepdims=True)
    out = jnp.einsum(
        "htl,lhc->thc", weights.astype(jnp.bfloat16), dec_vals, preferred_element_type=jnp.float32
    )
    read = readout.reshape(nheads, HEAD)
    onehot = (horizon_ids[:, None] == jnp.arange(HORIZONS, dtype=jnp.int32)[None, :]).astype(
        jnp.float32
    )
    target = jnp.sum(onehot * horizon_levels[None, :], axis=1)
    value_read = jnp.einsum("lhc,hc->hl", dec_vals.astype(jnp.float32), read, precision=high)
    lever = (
        weights
        * (
            value_read[:, None, :]
            - jnp.sum(value_read[:, None, :] * weights, axis=2, keepdims=True)
        )
    ).astype(jnp.bfloat16)
    pull = jnp.einsum("htl,lhc->thc", lever, dec_keys, preferred_element_type=jnp.float32) * scale
    field = pair_sum(jnp.sum(out * read[None, :, :], axis=(1, 2)), "heads", n_heads)
    miss = field - target
    dquery = (miss[:, None, None] * pull).reshape(count, local).astype(jnp.bfloat16)
    grad_query = lax.psum_scatter(
        jnp.dot(enc.T, dquery, preferred_element_type=jnp.float32).astype(jnp.bfloat16),
        "picks",
        scatter_dimension=0,
        tiled=True,
    ).astype(jnp.float32)
    return (field, latents_out, grad_query)


def solution(mesh):
    in_specs = (
        P(None, ("groups", "picks")),
        P(("groups", "picks")),
        P("groups"),
        P(),
        P("picks", None, "heads"),
        P("heads", None),
        P(),
        P(None, None, "heads"),
        P(None, "heads"),
        P(None, None, "heads"),
        P("picks", "heads"),
        P("heads"),
    )
    out_specs = (P(("groups", "picks")), P("groups", "heads"), P(("groups", "picks"), "heads"))
    body = functools.partial(
        on_device,
        n_picks=mesh.shape["picks"],
        n_heads=mesh.shape["heads"],
        n_groups=mesh.shape["groups"],
    )
    return jax.shard_map(body, mesh=mesh, in_specs=in_specs, out_specs=out_specs, check_vma=False)
```

profile of v0, /device:TPU:0, one launch (start us, length us, event | category | flops | bytes accessed | tf_op | source)
XLA Modules:
  0.0 216.1 jit_solution(17237952158772773728)
XLA Ops:
  9.2 2.4 %collective-permute-start = (bf16[256,1024]{1,0:T(8,128)(2,1)S(1)}, bf16[256,1024]{1,0:T(8,128)(2,1)S(1)}, u32[]{:S(2)}, u32[]{:S(2)}) collective-permute-start(bf16[256,1024]{1,0:T(8,128)(2,1)S(1)} %bitcast.124), channel_id=1, source_target_pairs={{0,3},{1,0},{2,1},{3,2},{4,7},{5,4},{6,5},{7,6},{8,11},{9,8},{10,9... | collective-permute-start | bytes 1572872 | tf_op jit(solution)/shard_map/ppermute | solution.py:30
  15.3 22.8 %fusion = (bf16[3,512,1024]{2,1,0:T(8,128)(2,1)S(1)}, bf16[3,512,1024]{2,1,0:T(8,128)(2,1)S(1)}) fusion(f32[3,1024]{1,0:T(4,128)S(1)} %copy-done.9, f32[512]{0:T(512)S(1)} %maximum_multiply_fusion), kind=kLoop, calls=%fused_computation.2 | loop fusion | flops 4718592 | bytes 6305792 | tf_op jit(solution)/shard_map/convert
  38.2 3.2 %pad_maximum_fusion = bf16[6,512,1024]{2,1,0:T(8,128)(2,1)} fusion(bf16[3,512,1024]{2,1,0:T(8,128)(2,1)S(1)} %get-tuple-element.29, bf16[3,512,1024]{2,1,0:T(8,128)(2,1)S(1)} %get-tuple-element.28), kind=kLoop, calls=%fused_computation.4 | loop fusion | flops 3145728 | bytes 12582912 | tf_op jit(solution)/shard_map/concatenate | solution.py:18
  41.4 5.1 %collective-permute-done.3 = bf16[256,1024]{1,0:T(8,128)(2,1)} collective-permute-done((bf16[256,1024]{1,0:T(8,128)(2,1)}, bf16[256,1024]{1,0:T(8,128)(2,1)}, u32[]{:S(2)}, u32[]{:S(2)}) %collective-permute-start.3) | collective-permute-done | bytes 524320 | tf_op jit(solution)/shard_map/ppermute | solution.py:30
  47.5 8.8 %collective-permute-done.4 = bf16[256,1024]{1,0:T(8,128)(2,1)} collective-permute-done((bf16[256,1024]{1,0:T(8,128)(2,1)}, bf16[256,1024]{1,0:T(8,128)(2,1)}, u32[]{:S(2)}, u32[]{:S(2)}) %collective-permute-start.4) | collective-permute-done | bytes 524320 | tf_op jit(solution)/shard_map/ppermute | solution.py:30
  56.3 5.1 %fusion.14 = bf16[4,256,1024]{2,1,0:T(8,128)(2,1)} fusion(s32[]{:T(128)S(6)} %select_n.27, bf16[1,256,1024]{2,1,0:T(8,128)(2,1)S(1)} %bitcast.143, bf16[1,256,1024]{2,1,0:T(8,128)(2,1)} %bitcast.13, bf16[1,256,1024]{2,1,0:T(8,128)(2,1)} %bitcast.14, bf16[1,256,1024]{2,1,0:T(8,128)(2,1)} %bitcast.15), kind=kLoop, calls=%fused_computation.38 | loop fusion | flops 7340032 | bytes 4194308 | tf_op jit(solution)/shard_map/jit(_roll_dynamic)/concatenate | solution.py:32
  61.4 14.5 %all-gather.6.cloned.1.call-done = bf16[3072,2,256]{2,1,0:T(2,128)(2,1)} async-done(((bf16[768,2,256]{2,1,0:T(2,128)(2,1)}), bf16[3072,2,256]{2,1,0:T(2,128)(2,1)}) %all-gather.6.cloned.1.call-update) | async-done | bytes 3145744 | tf_op jit(solution)/shard_map/all_gather | solution.py:89
  75.8 7.1 %fusion.32 = bf16[1024,2,256]{0,2,1:T(8,128)(2,1)S(1)} fusion(bf16[3072,1024,1]{1,0,2:T(8,128)(2,1)} %bitcast.118, bf16[3072,2,256]{2,1,0:T(2,128)(2,1)} %all-gather.6.cloned.1.call-done), kind=kOutput, calls=%fused_computation.81 | convolution fusion | flops 3221749760 | bytes 10485760 | tf_op jit(solution)/shard_map/tf,fjc->tjc/dot_general | solution.py:91
  83.9 2.0 copy-done.1
  87.9 4.8 %fusion.21 = bf16[4,256,1024]{2,1,0:T(8,128)(2,1)} fusion(s32[]{:T(128)S(6)} %select_n.27, bf16[1,256,1024]{2,1,0:T(8,128)(2,1)S(1)} %bitcast.127, bf16[1,256,1024]{2,1,0:T(8,128)(2,1)S(1)} %bitcast.144, bf16[1,256,1024]{2,1,0:T(8,128)(2,1)} %bitcast.5, bf16[1,256,1024]{2,1,0:T(8,128)(2,1)} %bitcast.6), kind=kLoop, calls=%fused_computation.45 | loop fusion | flops 7340032 | bytes 4194308 | tf_op jit(solution)/shard_map/jit(_roll_dynamic)/concatenate | solution.py:32
  93.6 13.3 %all-gather.1 = f32[8,2,512]{2,1,0:T(2,128)S(1)} all-gather(f32[2,2,512]{2,1,0:T(2,128)S(1)} %pad_maximum_fusion.1), channel_id=3, replica_groups=mesh['groups'=2,'picks'=4,'heads'=4] {'picks'}, dimensions={0}, use_global_device_ids=true | all-gather | bytes 40960 | tf_op jit(solution)/shard_map/all_gather | solution.py:105
  106.9 7.8 %all-gather.10.cloned.1.call-done = bf16[8,512,128]{2,1,0:T(8,128)(2,1)} async-done(((bf16[2,512,128]{2,1,0:T(8,128)(2,1)}), bf16[8,512,128]{2,1,0:T(8,128)(2,1)}) %all-gather.10.cloned.1.call-update) | async-done | bytes 1048592 | tf_op jit(solution)/shard_map/all_gather | solution.py:104
  114.7 1.8 multiply_reduce_fusion.2
  118.6 5.6 %collective-permute-done.6 = bf16[256,512]{1,0:T(8,128)(2,1)S(1)} collective-permute-done((bf16[256,512]{1,0:T(8,128)(2,1)S(1)}, bf16[256,512]{1,0:T(8,128)(2,1)S(1)}, u32[]{:S(2)}, u32[]{:S(2)}) %collective-permute-start.6) | collective-permute-done | bytes 262176 | tf_op jit(solution)/shard_map/ppermute | solution.py:30
  124.2 6.7 %collective-permute-done.7 = bf16[256,512]{1,0:T(8,128)(2,1)S(1)} collective-permute-done((bf16[256,512]{1,0:T(8,128)(2,1)S(1)}, bf16[256,512]{1,0:T(8,128)(2,1)S(1)}, u32[]{:S(2)}, u32[]{:S(2)}) %collective-permute-start.7) | collective-permute-done | bytes 262176 | tf_op jit(solution)/shard_map/ppermute | solution.py:30
  131.1 2.2 %fusion.60 = bf16[4,256,512]{2,1,0:T(8,128)(2,1)S(1)} fusion(s32[]{:T(128)S(6)} %select_n.27, bf16[1,256,512]{2,1,0:T(8,128)(2,1)S(1)} %bitcast.133, bf16[1,256,512]{2,1,0:T(8,128)(2,1)S(1)} %bitcast.147, bf16[1,256,512]{2,1,0:T(8,128)(2,1)S(1)} %bitcast.148, bf16[1,256,512]{2,1,0:T(8,128)(2,1)} %bitcast.32), kind=kLoop, calls=%fused_computation.103 | loop fusion | flops 3670016 | bytes 2097156 | tf_op jit(solution)/shard_map/jit(_roll_dynamic)/concatenate | solution.py:32
  138.9 4.0 %collective-permute-done.9 = bf16[256,512]{1,0:T(8,128)(2,1)S(1)} collective-permute-done((bf16[256,512]{1,0:T(8,128)(2,1)S(1)}, bf16[256,512]{1,0:T(8,128)(2,1)S(1)}, u32[]{:S(2)}, u32[]{:S(2)}) %collective-permute-start.9) | collective-permute-done | bytes 262176 | tf_op jit(solution)/shard_map/ppermute | solution.py:30
  142.9 8.3 %collective-permute-done.10 = bf16[256,512]{1,0:T(8,128)(2,1)S(1)} collective-permute-done((bf16[256,512]{1,0:T(8,128)(2,1)S(1)}, bf16[256,512]{1,0:T(8,128)(2,1)S(1)}, u32[]{:S(2)}, u32[]{:S(2)}) %collective-permute-start.10) | collective-permute-done | bytes 262176 | tf_op jit(solution)/shard_map/ppermute | solution.py:30
  156.3 5.1 %convolution_convert_fusion.2 = bf16[1024,256]{0,1:T(8,128)(2,1)S(1)} fusion(bf16[3072,1024]{1,0:T(8,128)(2,1)} %bitcast.119, bf16[3072,256]{1,0:T(8,128)(2,1)} %all-gather.8.cloned.1.call-done), kind=kOutput, calls=%fused_computation.84 | convolution fusion | flops 1610874880 | bytes 8388608 | tf_op jit(solution)/shard_map/dot_general | solution.py:153
  166.1 1.9 collective-permute-done.13
  170.2 3.1 %convolution_convert_fusion = bf16[3072,256]{1,0:T(8,128)(2,1)} fusion(bf16[3072,1024]{1,0:T(8,128)(2,1)S(1)} %bitcast.122, bf16[1024,256]{0,1:T(8,128)(2,1)S(1)} %bitcast.168), kind=kOutput, calls=%fused_computation.26 | convolution fusion | flops 1611399168 | bytes 8388608 | tf_op jit(solution)/shard_map/dot_general | solution.py:179
  173.4 1.9 constant_dynamic-slice_fusion
  175.2 32.4 %reduce-scatter.2.cloned.1.call-done = bf16[768,256]{1,0:T(8,128)(2,1)} async-done(((bf16[3072,256]{1,0:T(8,128)(2,1)}), bf16[768,256]{1,0:T(8,128)(2,1)}) %reduce-scatter.2.cloned.1.call-update) | async-done | bytes 393232 | tf_op jit(solution)/shard_map/reduce_scatter | solution.py:178
  207.6 1.9 convert_element_type.100
  (96 shorter events, 30.3 us)
Async XLA Ops:
  7.2 127.6 %copy-start = (bf16[3,1024,256]{2,1,0:T(8,128)(2,1)S(1)}, bf16[3,1024,256]{2,1,0:T(8,128)(2,1)}, u32[]{:S(2)}) copy-start(bf16[3,1024,256]{2,1,0:T(8,128)(2,1)} %param.23) | copy-start | bytes 4718596
  7.2 68.7 %all-gather.6.cloned.1.call-start = ((), (), s32[]{:S(2)}) async-start(), calls=%async_computation.1 | async-start | bytes 3932160 | tf_op jit(solution)/shard_map/all_gather | solution.py:89
  7.9 106.8 %all-gather.10.cloned.1.call-start = ((), (), s32[]{:S(2)}) async-start(), calls=%async_computation.4 | async-start | bytes 1310720 | tf_op jit(solution)/shard_map/all_gather | solution.py:104
  9.2 78.6 %collective-permute-start = (bf16[256,1024]{1,0:T(8,128)(2,1)S(1)}, bf16[256,1024]{1,0:T(8,128)(2,1)S(1)}, u32[]{:S(2)}, u32[]{:S(2)}) collective-permute-start(bf16[256,1024]{1,0:T(8,128)(2,1)S(1)} %bitcast.124), channel_id=1, source_target_pairs={{0,3},{1,0},{2,1},{3,2},{4,7},{5,4},{6,5},{7,6},{8,11},{9,8},{10,9... | collective-permute-start | bytes 1572872 | tf_op jit(solution)/shard_map/ppermute | solution.py:30
  11.7 76.2 %collective-permute-start.1 = (bf16[256,1024]{1,0:T(8,128)(2,1)S(1)}, bf16[256,1024]{1,0:T(8,128)(2,1)}, u32[]{:S(2)}, u32[]{:S(2)}) collective-permute-start(bf16[256,1024]{1,0:T(8,128)(2,1)S(1)} %bitcast.125), channel_id=1, source_target_pairs={{0,2},{1,3},{2,0},{3,1},{4,6},{5,7},{6,4},{7,5},{8,10},{9,11},{10,... | collective-permute-start | bytes 1572872 | tf_op jit(solution)/shard_map/ppermute | solution.py:30
  12.3 34.1 %collective-permute-start.3 = (bf16[256,1024]{1,0:T(8,128)(2,1)}, bf16[256,1024]{1,0:T(8,128)(2,1)}, u32[]{:S(2)}, u32[]{:S(2)}) collective-permute-start(bf16[256,1024]{1,0:T(8,128)(2,1)} %param.21), channel_id=1, source_target_pairs={{0,3},{1,0},{2,1},{3,2},{4,7},{5,4},{6,5},{7,6},{8,11},{9,8},{10,9... | collective-permute-start | bytes 1572872 | tf_op jit(solution)/shard_map/ppermute | solution.py:30
  12.4 43.9 %collective-permute-start.4 = (bf16[256,1024]{1,0:T(8,128)(2,1)}, bf16[256,1024]{1,0:T(8,128)(2,1)}, u32[]{:S(2)}, u32[]{:S(2)}) collective-permute-start(bf16[256,1024]{1,0:T(8,128)(2,1)} %param.21), channel_id=1, source_target_pairs={{0,2},{1,3},{2,0},{3,1},{4,6},{5,7},{6,4},{7,5},{8,10},{9,11},{10,... | collective-permute-start | bytes 1572872 | tf_op jit(solution)/shard_map/ppermute | solution.py:30
  14.1 42.2 %collective-permute-start.5 = (bf16[256,1024]{1,0:T(8,128)(2,1)}, bf16[256,1024]{1,0:T(8,128)(2,1)}, u32[]{:S(2)}, u32[]{:S(2)}) collective-permute-start(bf16[256,1024]{1,0:T(8,128)(2,1)} %param.21), channel_id=1, source_target_pairs={{0,1},{1,2},{2,3},{3,0},{4,5},{5,6},{6,7},{7,4},{8,9},{9,10},{10,1... | collective-permute-start | bytes 1572872 | tf_op jit(solution)/shard_map/ppermute | solution.py:30
  38.2 18.1 %copy-start.8 = (bf16[256,1024]{1,0:T(8,128)(2,1)S(1)}, bf16[256,1024]{1,0:T(8,128)(2,1)}, u32[]{:S(2)}) copy-start(bf16[256,1024]{1,0:T(8,128)(2,1)} %param.21) | copy-start | bytes 1572868
  46.4 41.4 %collective-permute-start.2 = (bf16[256,1024]{1,0:T(8,128)(2,1)S(1)}, bf16[256,1024]{1,0:T(8,128)(2,1)}, u32[]{:S(2)}, u32[]{:S(2)}) collective-permute-start(bf16[256,1024]{1,0:T(8,128)(2,1)S(1)} %bitcast.126), channel_id=1, source_target_pairs={{0,1},{1,2},{2,3},{3,0},{4,5},{5,6},{6,7},{7,4},{8,9},{9,10},{10,1... | collective-permute-start | bytes 1572872 | tf_op jit(solution)/shard_map/ppermute | solution.py:30
  87.6 68.7 %all-gather.8.cloned.1.call-start = ((), (), s32[]{:S(2)}) async-start(), calls=%async_computation.2 | async-start | bytes 1966080 | tf_op jit(solution)/shard_map/all_gather | solution.py:121
  93.5 24.9 %copy-start.10 = (f32[2,1024]{1,0:T(2,128)S(1)}, f32[2,1024]{1,0:T(2,128)}, u32[]{:S(2)}) copy-start(f32[2,1024]{1,0:T(2,128)} %param.22) | copy-start | bytes 24580
  116.7 16.7 %copy-start.6 = (bf16[512,1024]{1,0:T(8,128)(2,1)S(1)}, bf16[512,1024]{1,0:T(8,128)(2,1)}, u32[]{:S(2)}) copy-start(bf16[512,1024]{1,0:T(8,128)(2,1)} %param.19) | copy-start | bytes 3145732
  116.7 7.5 %collective-permute-start.6 = (bf16[256,512]{1,0:T(8,128)(2,1)S(1)}, bf16[256,512]{1,0:T(8,128)(2,1)S(1)}, u32[]{:S(2)}, u32[]{:S(2)}) collective-permute-start(bf16[256,512]{1,0:T(8,128)(2,1)S(1)} %bitcast.130), channel_id=1, source_target_pairs={{0,3},{1,0},{2,1},{3,2},{4,7},{5,4},{6,5},{7,6},{8,11},{9,8},{10,9... | collective-permute-start | bytes 786440 | tf_op jit(solution)/shard_map/ppermute | solution.py:30
  117.6 13.3 %collective-permute-start.7 = (bf16[256,512]{1,0:T(8,128)(2,1)S(1)}, bf16[256,512]{1,0:T(8,128)(2,1)S(1)}, u32[]{:S(2)}, u32[]{:S(2)}) collective-permute-start(bf16[256,512]{1,0:T(8,128)(2,1)S(1)} %bitcast.131), channel_id=1, source_target_pairs={{0,2},{1,3},{2,0},{3,1},{4,6},{5,7},{6,4},{7,5},{8,10},{9,11},{10,... | collective-permute-start | bytes 786440 | tf_op jit(solution)/shard_map/ppermute | solution.py:30
  118.3 12.8 %collective-permute-start.8 = (bf16[256,512]{1,0:T(8,128)(2,1)S(1)}, bf16[256,512]{1,0:T(8,128)(2,1)}, u32[]{:S(2)}, u32[]{:S(2)}) collective-permute-start(bf16[256,512]{1,0:T(8,128)(2,1)S(1)} %bitcast.132), channel_id=1, source_target_pairs={{0,1},{1,2},{2,3},{3,0},{4,5},{5,6},{6,7},{7,4},{8,9},{9,10},{10,1... | collective-permute-start | bytes 786440 | tf_op jit(solution)/shard_map/ppermute | solution.py:30
  118.5 89.1 %reduce-scatter.2.cloned.1.call-start = ((), (), s32[]{:S(2)}) async-start(), calls=%async_computation.3 | async-start | bytes 1966080 | tf_op jit(solution)/shard_map/reduce_scatter | solution.py:178
  118.6 14.8 %copy-start.3 = (bf16[4,256,1024]{2,1,0:T(8,128)(2,1)S(1)}, bf16[4,256,1024]{2,1,0:T(8,128)(2,1)}, u32[]{:S(2)}) copy-start(bf16[4,256,1024]{2,1,0:T(8,128)(2,1)} %fusion.14) | copy-start | bytes 6291460
  137.1 15.5 %copy-start.5 = (bf16[4,256,1024]{2,1,0:T(8,128)(2,1)S(1)}, bf16[4,256,1024]{2,1,0:T(8,128)(2,1)}, u32[]{:S(2)}) copy-start(bf16[4,256,1024]{2,1,0:T(8,128)(2,1)} %fusion.21) | copy-start | bytes 6291460
  137.1 5.8 %collective-permute-start.9 = (bf16[256,512]{1,0:T(8,128)(2,1)S(1)}, bf16[256,512]{1,0:T(8,128)(2,1)S(1)}, u32[]{:S(2)}, u32[]{:S(2)}) collective-permute-start(bf16[256,512]{1,0:T(8,128)(2,1)S(1)} %bitcast.149), channel_id=1, source_target_pairs={{0,3},{1,0},{2,1},{3,2},{4,7},{5,4},{6,5},{7,6},{8,11},{9,8},{10,9... | collective-permute-start | bytes 786440 | tf_op jit(solution)/shard_map/ppermute | solution.py:30
  137.1 14.0 %collective-permute-start.10 = (bf16[256,512]{1,0:T(8,128)(2,1)S(1)}, bf16[256,512]{1,0:T(8,128)(2,1)S(1)}, u32[]{:S(2)}, u32[]{:S(2)}) collective-permute-start(bf16[256,512]{1,0:T(8,128)(2,1)S(1)} %bitcast.150), channel_id=1, source_target_pairs={{0,2},{1,3},{2,0},{3,1},{4,6},{5,7},{6,4},{7,5},{8,10},{9,11},{10,... | collective-permute-start | bytes 786440 | tf_op jit(solution)/shard_map/ppermute | solution.py:30
  138.6 12.7 %collective-permute-start.11 = (bf16[256,512]{1,0:T(8,128)(2,1)S(1)}, bf16[256,512]{1,0:T(8,128)(2,1)S(1)}, u32[]{:S(2)}, u32[]{:S(2)}) collective-permute-start(bf16[256,512]{1,0:T(8,128)(2,1)S(1)} %bitcast.151), channel_id=1, source_target_pairs={{0,1},{1,2},{2,3},{3,0},{4,5},{5,6},{6,7},{7,4},{8,9},{9,10},{10,1... | collective-permute-start | bytes 786440 | tf_op jit(solution)/shard_map/ppermute | solution.py:30
  163.2 1.2 collective-permute-start.12
  164.4 3.6 %collective-permute-start.13 = (f32[1024]{0:T(1024)S(1)}, f32[1024]{0:T(1024)S(1)}, u32[]{:S(2)}, u32[]{:S(2)}) collective-permute-start(f32[1024]{0:T(1024)S(1)} %add.61), channel_id=1, source_target_pairs={{0,2},{1,3},{2,0},{3,1},{4,6},{5,7},{6,4},{7,5},{8,10},{9,11},{10,... | collective-permute-start | bytes 12296 | tf_op jit(solution)/shard_map/ppermute | solution.py:58
  (10 other events, 30.6 us)
Sparse Core Ops, SparseCore 0:
  9.6 66.2 all-gather.5
  87.7 26.9 all-gather.9
  118.7 36.9 all-gather.7
  173.5 34.0 reduce-scatter.1
where the time goes:
time: 216 us
  waiting for transfers between devices  97 us (45%)
  other arithmetic  45.7 us (21%)
  matrix products  26.8 us (12%)
  between operations  14.2 us (7%)
  blocking collectives  13.3 us (6%)
  starting transfers between devices  10.7 us (5%)
  local copies, waits for them, and re-layouts  8.39 us (4%)
    ppermute x12, waiting for transfers between devices, ring_gather(): blocks.append(lax.ppermute(x, axis, [(i, (i - s) % n) for i in range(n)]))  38.8 us
    reduce_scatter x1, waiting for transfers between devices, on_device(): lax.psum_scatter(jnp.dot(enc.T, dquery, preferred_element_type=jnp.float3...  32.4 us
    another operation x1, other arithmetic  22.8 us
    all_gather x1, waiting for transfers between devices, on_device(): piece = lax.all_gather(kv_weight, 'picks', axis=0, tiled=True)  14.5 us
    concatenate x4, other arithmetic, ring_gather(): ordered = jnp.roll(flipped, idx, axis=0)  13.3 us
    all_gather x1, blocking collectives, on_device(): lax.all_gather(jnp.stack([top, total]), 'picks', axis=0, tiled=False)  13.3 us
    ppermute x12, starting transfers between devices, ring_gather(): blocks.append(lax.ppermute(x, axis, [(i, (i - s) % n) for i in range(n)]))  9.4 us
    all_gather x1, waiting for transfers between devices, on_device(): lax.all_gather(numer.astype(jnp.bfloat16), 'picks', axis=0, tiled=False)  7.77 us
  transfers between devices with their start and end apart: 18, of which 13 were waited for; matrix products, arithmetic and copies ran while one was open for 28% of the time, Pallas kernels for 0%

commit v1 on v0

--- a/solution.py
+++ b/solution.py
@@ -86,7 +86,20 @@
     column = lax.axis_index("heads") * local
     enc = encode(coords)
     cross_full = ring_gather(cross_out, "heads", n_heads)
-    piece = lax.all_gather(kv_weight, "picks", axis=0, tiled=True)
+    original = kv_weight
+    front = jax.lax.axis_size("picks")
+    mid_arr = jax.lax.axis_index("picks")
+    spare, z1, arr_next = (front, mid_arr, original.shape[0])
+    slots = [b * spare if ii == 0 else b for ii, b in enumerate(original.shape)]
+    odd = jnp.zeros(slots, original.dtype)
+    piece = lax.dynamic_update_slice_in_dim(odd, original, z1 * arr_next, axis=0)
+    for src_i in range(1, spare):
+        original = jax.lax.ppermute(
+            original, axis_name="picks", perm=[(ii, (ii + 1) % spare) for ii in range(spare)]
+        )
+        piece = lax.dynamic_update_slice_in_dim(
+            piece, original, (z1 - src_i) % spare * arr_next, axis=0
+        )
     cross_full, piece = lax.optimization_barrier((cross_full, piece))
     keys_vals = jnp.einsum("tf,fjc->tjc", enc, piece, preferred_element_type=jnp.float32).astype(
         jnp.bfloat16

time: 216 us -> 232 us (1.074)
  local copies, waits for them, and re-layouts: 8.39 us -> 23.3 us
  waiting for transfers between devices: 97 us -> 90.3 us
  starting transfers between devices: 10.7 us -> 13.7 us
  other arithmetic: 45.7 us -> 48.6 us
    ppermute x0 -> x3, waiting for transfers between devices: none -> 22.6 us  [on_device(): jax.lax.ppermute(original, axis_name='picks', perm=[(ii, (ii + 1) % spare...]
    all_gather x1 -> x0, waiting for transfers between devices: 14.5 us -> none  [on_device(): piece = lax.all_gather(kv_weight, 'picks', axis=0, tiled=True)]
    ppermute x12, waiting for transfers between devices: 38.8 us -> 24.9 us  [ring_gather(): blocks.append(lax.ppermute(x, axis, [(i, (i - s) % n) for i in range(n)]))]
    ppermute x0 -> x3, local copies, waits for them, and re-layouts: none -> 6.68 us  [on_device(): jax.lax.ppermute(original, axis_name='picks', perm=[(ii, (ii + 1) % spare...]
    unnamed x34 -> x39, local copies, waits for them, and re-layouts: 5.17 us -> 9.87 us
    ppermute x0 -> x3, starting transfers between devices: none -> 4.42 us  [on_device(): jax.lax.ppermute(original, axis_name='picks', perm=[(ii, (ii + 1) % spare...]
    dynamic_update_slice x0 -> x4, local copies, waits for them, and re-layouts: none -> 3.18 us  [the longest x3 3.08 us: on_device(): lax.dynamic_update_slice_in_dim(piece, original, (z1 - src_i) % spare * a...]
  transfers between devices with their start and end apart: 18 -> 20, of which waited for: 13 -> 12; matrix products, arithmetic and copies ran while one was open for 28% -> 34% of each run, Pallas kernels for 0% -> 0%
where the time goes in v1:
time: 232 us; the launch traced here: 231 us
  waiting for transfers between devices  90.3 us (39%)
  other arithmetic  48.6 us (21%)
  matrix products  28 us (12%)
  local copies, waits for them, and re-layouts  23.3 us (10%)
  between operations  14.2 us (6%)
  starting transfers between devices  13.7 us (6%)
  blocking collectives  13.2 us (6%)
    reduce_scatter x1, waiting for transfers between devices, on_device(): lax.psum_scatter(jnp.dot(enc.T, dquery, preferred_element_type=jnp.float3...  32.4 us
    ppermute x12, waiting for transfers between devices, ring_gather(): blocks.append(lax.ppermute(x, axis, [(i, (i - s) % n) for i in range(n)]))  24.9 us
    another operation x1, other arithmetic  24.5 us
    ppermute x3, waiting for transfers between devices, on_device(): jax.lax.ppermute(original, axis_name='picks', perm=[(ii, (ii + 1) % spare...  22.6 us
    all_gather x1, blocking collectives, on_device(): lax.all_gather(jnp.stack([top, total]), 'picks', axis=0, tiled=False)  13.2 us
    concatenate x4, other arithmetic, ring_gather(): ordered = jnp.roll(flipped, idx, axis=0)  12.6 us
    unnamed x39, local copies, waits for them, and re-layouts  9.87 us
    ppermute x12, starting transfers between devices, ring_gather(): blocks.append(lax.ppermute(x, axis, [(i, (i - s) % n) for i in range(n)]))  8.17 us
  transfers between devices with their start and end apart: 20, of which 12 were waited for; matrix products, arithmetic and copies ran while one was open for 34% of the time, Pallas kernels for 0%

profile of v1, /device:TPU:0, one launch (start us, length us, event | category | flops | bytes accessed | tf_op | source)
XLA Modules:
  0.0 231.4 jit_solution(8625089884025920528)
XLA Ops:
  7.2 3.1 %collective-permute-start.6 = (bf16[768,2,256]{2,1,0:T(2,128)(2,1)}, bf16[768,2,256]{2,1,0:T(2,128)(2,1)}, u32[]{:S(2)}, u32[]{:S(2)}) collective-permute-start(bf16[768,2,256]{2,1,0:T(2,128)(2,1)} %param.20), channel_id=1, source_target_pairs={{0,4},{4,8},{8,12},{12,0},{1,5},{5,9},{9,13},{13,1},{2,6},{6,10},{... | collective-permute-start | bytes 2359304 | tf_op jit(solution)/shard_map/ppermute | solution.py:97
  14.9 2.2 copy.71
  17.2 13.0 %collective-permute-done.6 = bf16[768,2,256]{2,1,0:T(2,128)(2,1)} collective-permute-done((bf16[768,2,256]{2,1,0:T(2,128)(2,1)}, bf16[768,2,256]{2,1,0:T(2,128)(2,1)}, u32[]{:S(2)}, u32[]{:S(2)}) %collective-permute-start.6) | collective-permute-done | bytes 786464 | tf_op jit(solution)/shard_map/ppermute | solution.py:97
  30.2 24.5 %fusion = (bf16[3,512,1024]{2,1,0:T(8,128)(2,1)}, bf16[3,512,1024]{2,1,0:T(8,128)(2,1)}) fusion(f32[3,1024]{1,0:T(4,128)S(1)} %copy-done.11, f32[512]{0:T(512)S(1)} %maximum_multiply_fusion), kind=kLoop, calls=%fused_computation.2 | loop fusion | flops 4718592 | bytes 6305792 | tf_op jit(solution)/shard_map/convert
  56.3 2.5 %copy-done.4 = bf16[3,512,1024]{2,1,0:T(8,128)(2,1)S(1)} copy-done((bf16[3,512,1024]{2,1,0:T(8,128)(2,1)S(1)}, bf16[3,512,1024]{2,1,0:T(8,128)(2,1)}, u32[]{:S(2)}) %copy-start.4) | copy-done | bytes 3145752
  58.8 5.2 %pad_maximum_fusion = bf16[6,512,1024]{2,1,0:T(8,128)(2,1)} fusion(bf16[3,512,1024]{2,1,0:T(8,128)(2,1)} %get-tuple-element.29, bf16[3,512,1024]{2,1,0:T(8,128)(2,1)S(1)} %copy-done.4), kind=kLoop, calls=%fused_computation.4 | loop fusion | flops 3145728 | bytes 12582912 | tf_op jit(solution)/shard_map/concatenate | solution.py:18
  66.8 5.0 %fusion.12 = bf16[4,256,1024]{2,1,0:T(8,128)(2,1)} fusion(s32[]{:T(128)S(6)} %select_n.60, bf16[1,256,1024]{2,1,0:T(8,128)(2,1)S(1)} %bitcast.144, bf16[1,256,1024]{2,1,0:T(8,128)(2,1)} %bitcast.13, bf16[1,256,1024]{2,1,0:T(8,128)(2,1)} %bitcast.14, bf16[1,256,1024]{2,1,0:T(8,128)(2,1)} %bitcast.15), kind=kLoop, calls=%fused_computation.36 | loop fusion | flops 7340032 | bytes 4194308 | tf_op jit(solution)/shard_map/jit(_roll_dynamic)/concatenate | solution.py:32
  71.8 2.2 copy.72
  75.1 2.2 copy.73
  78.3 9.6 %collective-permute-done.8 = bf16[768,2,256]{2,1,0:T(2,128)(2,1)} collective-permute-done((bf16[768,2,256]{2,1,0:T(2,128)(2,1)}, bf16[768,2,256]{2,1,0:T(2,128)(2,1)}, u32[]{:S(2)}, u32[]{:S(2)}) %collective-permute-start.8) | collective-permute-done | bytes 786464 | tf_op jit(solution)/shard_map/ppermute | solution.py:97
  87.9 2.2 copy.74
  91.2 7.1 %convolution_convert_fusion.1 = bf16[1024,2,256]{0,2,1:T(8,128)(2,1)S(1)} fusion(bf16[3072,1024,1]{1,0,2:T(8,128)(2,1)} %bitcast.119, bf16[3072,2,256]{0,2,1:T(8,128)(2,1)} %constant_dynamic-update-slice_fusion), kind=kOutput, calls=%fused_computation.79 | convolution fusion | flops 3221749760 | bytes 10485760 | tf_op jit(solution)/shard_map/tf,fjc->tjc/dot_general | solution.py:104
  99.3 2.0 copy-done.2
  103.2 5.1 %fusion.19 = bf16[4,256,1024]{2,1,0:T(8,128)(2,1)} fusion(s32[]{:T(128)S(6)} %select_n.60, bf16[1,256,1024]{2,1,0:T(8,128)(2,1)S(1)} %bitcast.128, bf16[1,256,1024]{2,1,0:T(8,128)(2,1)} %bitcast.4, bf16[1,256,1024]{2,1,0:T(8,128)(2,1)} %bitcast.5, bf16[1,256,1024]{2,1,0:T(8,128)(2,1)} %bitcast.6), kind=kLoop, calls=%fused_computation.43 | loop fusion | flops 7340032 | bytes 4194308 | tf_op jit(solution)/shard_map/jit(_roll_dynamic)/concatenate | solution.py:32
  109.2 13.2 %all-gather.1 = f32[8,2,512]{2,1,0:T(2,128)S(1)} all-gather(f32[2,2,512]{2,1,0:T(2,128)S(1)} %pad_maximum_fusion.1), channel_id=3, replica_groups=mesh['groups'=2,'picks'=4,'heads'=4] {'picks'}, dimensions={0}, use_global_device_ids=true | all-gather | bytes 40960 | tf_op jit(solution)/shard_map/all_gather | solution.py:118
  122.5 7.4 %all-gather.7.cloned.1.call-done = bf16[8,512,128]{2,1,0:T(8,128)(2,1)} async-done(((bf16[2,512,128]{2,1,0:T(8,128)(2,1)}), bf16[8,512,128]{2,1,0:T(8,128)(2,1)}) %all-gather.7.cloned.1.call-update) | async-done | bytes 1048592 | tf_op jit(solution)/shard_map/all_gather | solution.py:117
  133.8 5.5 %collective-permute-done.9 = bf16[256,512]{1,0:T(8,128)(2,1)S(1)} collective-permute-done((bf16[256,512]{1,0:T(8,128)(2,1)S(1)}, bf16[256,512]{1,0:T(8,128)(2,1)S(1)}, u32[]{:S(2)}, u32[]{:S(2)}) %collective-permute-start.9) | collective-permute-done | bytes 262176 | tf_op jit(solution)/shard_map/ppermute | solution.py:30
  139.3 6.8 %collective-permute-done.10 = bf16[256,512]{1,0:T(8,128)(2,1)S(1)} collective-permute-done((bf16[256,512]{1,0:T(8,128)(2,1)S(1)}, bf16[256,512]{1,0:T(8,128)(2,1)S(1)}, u32[]{:S(2)}, u32[]{:S(2)}) %collective-permute-start.10) | collective-permute-done | bytes 262176 | tf_op jit(solution)/shard_map/ppermute | solution.py:30
  147.4 2.6 %multiply_reduce_fusion.4 = (f32[512]{0:T(512)S(1)}, f32[512,1024]{1,0:T(8,128)S(1)}) fusion(bf16[1024,512]{1,0:T(8,128)(2,1)S(1)} %bitcast.124, bf16[1024,1024]{1,0:T(8,128)(2,1)S(1)} %bitcast.118, bf16[512,1024]{1,0:T(8,128)(2,1)} %param.19), kind=kOutput, calls=%fused_computation.73 | convolution fusion | flops 1075838464 | bytes 6293504 | tf_op jit(solution)/shard_map/dot_general | solution.py:136
  154.1 4.1 %collective-permute-done.12 = bf16[256,512]{1,0:T(8,128)(2,1)S(1)} collective-permute-done((bf16[256,512]{1,0:T(8,128)(2,1)S(1)}, bf16[256,512]{1,0:T(8,128)(2,1)S(1)}, u32[]{:S(2)}, u32[]{:S(2)}) %collective-permute-start.12) | collective-permute-done | bytes 262176 | tf_op jit(solution)/shard_map/ppermute | solution.py:30
  158.2 8.2 %collective-permute-done.13 = bf16[256,512]{1,0:T(8,128)(2,1)S(1)} collective-permute-done((bf16[256,512]{1,0:T(8,128)(2,1)S(1)}, bf16[256,512]{1,0:T(8,128)(2,1)S(1)}, u32[]{:S(2)}, u32[]{:S(2)}) %collective-permute-start.13) | collective-permute-done | bytes 262176 | tf_op jit(solution)/shard_map/ppermute | solution.py:30
  171.5 5.1 %convolution_convert_fusion.3 = bf16[1024,256]{0,1:T(8,128)(2,1)S(1)} fusion(bf16[3072,1024]{1,0:T(8,128)(2,1)} %bitcast.120, bf16[3072,256]{1,0:T(8,128)(2,1)} %all-gather.5.cloned.1.call-done), kind=kOutput, calls=%fused_computation.82 | convolution fusion | flops 1610874880 | bytes 8388608 | tf_op jit(solution)/shard_map/dot_general | solution.py:166
  185.4 3.1 %convolution_convert_fusion = bf16[3072,256]{1,0:T(8,128)(2,1)} fusion(bf16[3072,1024]{1,0:T(8,128)(2,1)S(1)} %bitcast.123, bf16[1024,256]{0,1:T(8,128)(2,1)S(1)} %bitcast.169), kind=kOutput, calls=%fused_computation.26 | convolution fusion | flops 1611399168 | bytes 8388608 | tf_op jit(solution)/shard_map/dot_general | solution.py:192
  190.5 32.4 %reduce-scatter.2.cloned.1.call-done = bf16[768,256]{1,0:T(8,128)(2,1)} async-done(((bf16[3072,256]{1,0:T(8,128)(2,1)}), bf16[768,256]{1,0:T(8,128)(2,1)}) %reduce-scatter.2.cloned.1.call-update) | async-done | bytes 393232 | tf_op jit(solution)/shard_map/reduce_scatter | solution.py:191
  (112 shorter events, 42.9 us)
Async XLA Ops:
  7.2 142.9 %copy-start = (bf16[3,1024,256]{2,1,0:T(8,128)(2,1)S(1)}, bf16[3,1024,256]{2,1,0:T(8,128)(2,1)}, u32[]{:S(2)}) copy-start(bf16[3,1024,256]{2,1,0:T(8,128)(2,1)} %param.23) | copy-start | bytes 4718596
  7.2 23.0 %copy-start.11 = (f32[3,1024]{1,0:T(4,128)S(1)}, f32[3,1024]{1,0:T(4,128)}, u32[]{:S(2)}) copy-start(f32[3,1024]{1,0:T(4,128)} %param.16) | copy-start | bytes 36868
  7.2 122.7 %all-gather.7.cloned.1.call-start = ((), (), s32[]{:S(2)}) async-start(), calls=%async_computation.3 | async-start | bytes 1310720 | tf_op jit(solution)/shard_map/all_gather | solution.py:117
  7.2 23.0 %collective-permute-start.6 = (bf16[768,2,256]{2,1,0:T(2,128)(2,1)}, bf16[768,2,256]{2,1,0:T(2,128)(2,1)}, u32[]{:S(2)}, u32[]{:S(2)}) collective-permute-start(bf16[768,2,256]{2,1,0:T(2,128)(2,1)} %param.20), channel_id=1, source_target_pairs={{0,4},{4,8},{8,12},{12,0},{1,5},{5,9},{9,13},{13,1},{2,6},{6,10},{... | collective-permute-start | bytes 2359304 | tf_op jit(solution)/shard_map/ppermute | solution.py:97
  10.3 53.6 %collective-permute-start.3 = (bf16[256,1024]{1,0:T(8,128)(2,1)}, bf16[256,1024]{1,0:T(8,128)(2,1)}, u32[]{:S(2)}, u32[]{:S(2)}) collective-permute-start(bf16[256,1024]{1,0:T(8,128)(2,1)} %param.21), channel_id=1, source_target_pairs={{0,3},{1,0},{2,1},{3,2},{4,7},{5,4},{6,5},{7,6},{8,11},{9,8},{10,9... | collective-permute-start | bytes 1572872 | tf_op jit(solution)/shard_map/ppermute | solution.py:30
  11.0 54.5 %collective-permute-start.4 = (bf16[256,1024]{1,0:T(8,128)(2,1)}, bf16[256,1024]{1,0:T(8,128)(2,1)}, u32[]{:S(2)}, u32[]{:S(2)}) collective-permute-start(bf16[256,1024]{1,0:T(8,128)(2,1)} %param.21), channel_id=1, source_target_pairs={{0,2},{1,3},{2,0},{3,1},{4,6},{5,7},{6,4},{7,5},{8,10},{9,11},{10,... | collective-permute-start | bytes 1572872 | tf_op jit(solution)/shard_map/ppermute | solution.py:30
  11.8 55.0 %collective-permute-start.5 = (bf16[256,1024]{1,0:T(8,128)(2,1)}, bf16[256,1024]{1,0:T(8,128)(2,1)}, u32[]{:S(2)}, u32[]{:S(2)}) collective-permute-start(bf16[256,1024]{1,0:T(8,128)(2,1)} %param.21), channel_id=1, source_target_pairs={{0,1},{1,2},{2,3},{3,0},{4,5},{5,6},{6,7},{7,4},{8,9},{9,10},{10,1... | collective-permute-start | bytes 1572872 | tf_op jit(solution)/shard_map/ppermute | solution.py:30
  13.3 89.9 %collective-permute-start = (bf16[256,1024]{1,0:T(8,128)(2,1)S(1)}, bf16[256,1024]{1,0:T(8,128)(2,1)}, u32[]{:S(2)}, u32[]{:S(2)}) collective-permute-start(bf16[256,1024]{1,0:T(8,128)(2,1)S(1)} %bitcast.125), channel_id=1, source_target_pairs={{0,3},{1,0},{2,1},{3,2},{4,7},{5,4},{6,5},{7,6},{8,11},{9,8},{10,9... | collective-permute-start | bytes 1572872 | tf_op jit(solution)/shard_map/ppermute | solution.py:30
  30.2 35.3 %collective-permute-start.7 = (bf16[768,2,256]{2,1,0:T(2,128)(2,1)}, bf16[768,2,256]{2,1,0:T(2,128)(2,1)}, u32[]{:S(2)}, u32[]{:S(2)}) collective-permute-start(bf16[768,2,256]{2,1,0:T(2,128)(2,1)} %collective-permute-done.6), channel_id=1, source_target_pairs={{0,4},{4,8},{8,12},{12,0},{1,5},{5,9},{9,13},{13,1},{2,6},{6,10},{... | collective-permute-start | bytes 2359304 | tf_op jit(solution)/shard_map/ppermute | solution.py:97
  64.0 39.2 %collective-permute-start.1 = (bf16[256,1024]{1,0:T(8,128)(2,1)S(1)}, bf16[256,1024]{1,0:T(8,128)(2,1)}, u32[]{:S(2)}, u32[]{:S(2)}) collective-permute-start(bf16[256,1024]{1,0:T(8,128)(2,1)S(1)} %bitcast.126), channel_id=1, source_target_pairs={{0,2},{1,3},{2,0},{3,1},{4,6},{5,7},{6,4},{7,5},{8,10},{9,11},{10,... | collective-permute-start | bytes 1572872 | tf_op jit(solution)/shard_map/ppermute | solution.py:30
  65.4 37.7 %collective-permute-start.2 = (bf16[256,1024]{1,0:T(8,128)(2,1)S(1)}, bf16[256,1024]{1,0:T(8,128)(2,1)}, u32[]{:S(2)}, u32[]{:S(2)}) collective-permute-start(bf16[256,1024]{1,0:T(8,128)(2,1)S(1)} %bitcast.127), channel_id=1, source_target_pairs={{0,1},{1,2},{2,3},{3,0},{4,5},{5,6},{6,7},{7,4},{8,9},{9,10},{10,1... | collective-permute-start | bytes 1572872 | tf_op jit(solution)/shard_map/ppermute | solution.py:30
  65.5 22.5 %collective-permute-start.8 = (bf16[768,2,256]{2,1,0:T(2,128)(2,1)}, bf16[768,2,256]{2,1,0:T(2,128)(2,1)}, u32[]{:S(2)}, u32[]{:S(2)}) collective-permute-start(bf16[768,2,256]{2,1,0:T(2,128)(2,1)} %collective-permute-done.7), channel_id=1, source_target_pairs={{0,4},{4,8},{8,12},{12,0},{1,5},{5,9},{9,13},{13,1},{2,6},{6,10},{... | collective-permute-start | bytes 2359304 | tf_op jit(solution)/shard_map/ppermute | solution.py:97
  102.9 68.6 %all-gather.5.cloned.1.call-start = ((), (), s32[]{:S(2)}) async-start(), calls=%async_computation.1 | async-start | bytes 1966080 | tf_op jit(solution)/shard_map/all_gather | solution.py:134
  109.2 24.5 %copy-start.12 = (f32[2,1024]{1,0:T(2,128)S(1)}, f32[2,1024]{1,0:T(2,128)}, u32[]{:S(2)}) copy-start(f32[2,1024]{1,0:T(2,128)} %param.22) | copy-start | bytes 24580
  131.9 7.3 %collective-permute-start.9 = (bf16[256,512]{1,0:T(8,128)(2,1)S(1)}, bf16[256,512]{1,0:T(8,128)(2,1)S(1)}, u32[]{:S(2)}, u32[]{:S(2)}) collective-permute-start(bf16[256,512]{1,0:T(8,128)(2,1)S(1)} %bitcast.131), channel_id=1, source_target_pairs={{0,3},{1,0},{2,1},{3,2},{4,7},{5,4},{6,5},{7,6},{8,11},{9,8},{10,9... | collective-permute-start | bytes 786440 | tf_op jit(solution)/shard_map/ppermute | solution.py:30
  132.8 13.3 %collective-permute-start.10 = (bf16[256,512]{1,0:T(8,128)(2,1)S(1)}, bf16[256,512]{1,0:T(8,128)(2,1)S(1)}, u32[]{:S(2)}, u32[]{:S(2)}) collective-permute-start(bf16[256,512]{1,0:T(8,128)(2,1)S(1)} %bitcast.132), channel_id=1, source_target_pairs={{0,2},{1,3},{2,0},{3,1},{4,6},{5,7},{6,4},{7,5},{8,10},{9,11},{10,... | collective-permute-start | bytes 786440 | tf_op jit(solution)/shard_map/ppermute | solution.py:30
  133.5 12.7 %collective-permute-start.11 = (bf16[256,512]{1,0:T(8,128)(2,1)S(1)}, bf16[256,512]{1,0:T(8,128)(2,1)S(1)}, u32[]{:S(2)}, u32[]{:S(2)}) collective-permute-start(bf16[256,512]{1,0:T(8,128)(2,1)S(1)} %bitcast.133), channel_id=1, source_target_pairs={{0,1},{1,2},{2,3},{3,0},{4,5},{5,6},{6,7},{7,4},{8,9},{9,10},{10,1... | collective-permute-start | bytes 786440 | tf_op jit(solution)/shard_map/ppermute | solution.py:30
  133.7 89.2 %reduce-scatter.2.cloned.1.call-start = ((), (), s32[]{:S(2)}) async-start(), calls=%async_computation.2 | async-start | bytes 1966080 | tf_op jit(solution)/shard_map/reduce_scatter | solution.py:191
  152.4 5.8 %collective-permute-start.12 = (bf16[256,512]{1,0:T(8,128)(2,1)S(1)}, bf16[256,512]{1,0:T(8,128)(2,1)S(1)}, u32[]{:S(2)}, u32[]{:S(2)}) collective-permute-start(bf16[256,512]{1,0:T(8,128)(2,1)S(1)} %bitcast.149), channel_id=1, source_target_pairs={{0,3},{1,0},{2,1},{3,2},{4,7},{5,4},{6,5},{7,6},{8,11},{9,8},{10,9... | collective-permute-start | bytes 786440 | tf_op jit(solution)/shard_map/ppermute | solution.py:30
  152.4 13.9 %collective-permute-start.13 = (bf16[256,512]{1,0:T(8,128)(2,1)S(1)}, bf16[256,512]{1,0:T(8,128)(2,1)S(1)}, u32[]{:S(2)}, u32[]{:S(2)}) collective-permute-start(bf16[256,512]{1,0:T(8,128)(2,1)S(1)} %bitcast.150), channel_id=1, source_target_pairs={{0,2},{1,3},{2,0},{3,1},{4,6},{5,7},{6,4},{7,5},{8,10},{9,11},{10,... | collective-permute-start | bytes 786440 | tf_op jit(solution)/shard_map/ppermute | solution.py:30
  153.9 12.7 %collective-permute-start.14 = (bf16[256,512]{1,0:T(8,128)(2,1)S(1)}, bf16[256,512]{1,0:T(8,128)(2,1)S(1)}, u32[]{:S(2)}, u32[]{:S(2)}) collective-permute-start(bf16[256,512]{1,0:T(8,128)(2,1)S(1)} %bitcast.151), channel_id=1, source_target_pairs={{0,1},{1,2},{2,3},{3,0},{4,5},{5,6},{6,7},{7,4},{8,9},{9,10},{10,1... | collective-permute-start | bytes 786440 | tf_op jit(solution)/shard_map/ppermute | solution.py:30
  178.4 1.2 collective-permute-start.15
  179.6 3.6 %collective-permute-start.16 = (f32[1024]{0:T(1024)S(1)}, f32[1024]{0:T(1024)S(1)}, u32[]{:S(2)}, u32[]{:S(2)}) collective-permute-start(f32[1024]{0:T(1024)S(1)} %add.93), channel_id=1, source_target_pairs={{0,2},{1,3},{2,0},{3,1},{4,6},{5,7},{6,4},{7,5},{8,10},{9,11},{10,... | collective-permute-start | bytes 12296 | tf_op jit(solution)/shard_map/ppermute | solution.py:58
  185.4 39.4 %copy-start.1 = (bf16[3,1024,256]{2,1,0:T(8,128)(2,1)S(1)}, bf16[3,1024,256]{2,1,0:T(8,128)(2,1)}, u32[]{:S(2)}) copy-start(bf16[3,1024,256]{2,1,0:T(8,128)(2,1)} %param.23) | copy-start | bytes 4718596
  (14 other events, 70.6 us)
Sparse Core Ops, SparseCore 0:
  103.0 26.8 all-gather.6
  133.8 36.9 all-gather.4
  188.7 34.1 reduce-scatter.1
